TPU v7x, 512 devices: a whole 4x8x8 slice. The times are simulated.
512 devices in a mesh: req: 64 (over z, x, core), tp: 8 (over y).
Axes of the slice: x: 4, y: 8, z: 8, core: 2. Of those that a mesh axis runs over, the one named last changes fastest.
Arguments:
- q_new: bfloat16 [4096, 5120], P('req', 'tp'), may hold values from -6 to 6
- k_new: bfloat16 [4096, 1024], P('req', 'tp'), may hold values from -15 to 15
- v_new: bfloat16 [4096, 1024], P('req', 'tp'), may hold values from -6 to 6
- k_cache: bfloat16 [1024, 128, 1024], P('req', None, 'tp'), may hold values from -16 to 16
- v_cache: bfloat16 [1024, 128, 1024], P('req', None, 'tp'), may hold values from -6 to 6
- lengths: int32 [32], replicated, may hold values from 1 to 4096, as said below
- page_table: int32 [32, 32], replicated, may hold values from -1 to 1023, as said below
- w_out: bfloat16 [5120, 5120], P('req', 'tp'), may hold values from -0.078125 to 0.078125
Outputs:
- attn_out: bfloat16 [4096, 5120], P('req')
Inputs may be any that keep to these rules, and one draw needn't show every extreme that they name: `lengths`: the last request, 31, has exactly 4096 cached tokens; every request has at least one. `page_table`: request r uses ceil(lengths[r] / 128) logical pages. Its first ceil(ceil(lengths[r] / 128) / 2) logical pages lie among global pages 2r * 16 to (2r + 1) * 16 - 1, the rest among (2r + 1) * 16 to (2r + 2) * 16 - 1; distinct logical pages use distinct global pages; entries past a request's last page are -1.
All inputs are finite; a program needn't handle non-finite values.
Results may differ from a plain program's by a relative error of at most 0.024.
Values may be sent and summed in bfloat16 or wider, within the bound.
No kernel may reach another device: no remote copies, remote signals or barrier semaphores. Data moves between devices by JAX's collectives and lax.ppermute only.
A program may use at most 64 MiB of HBM per device.

v0:
```python
import math
import jax
import jax.numpy as jnp
from jax import lax
from jax.sharding import PartitionSpec as P

HD = 128
GROUP = 5
BLOCK_PAGES = 4
ROPE_BASE = 1000000.0
FLOOR_SCORE = -1e30


def from_partner(value, axis, distance):
    return lax.ppermute(value, axis, [(i, i ^ 1 << distance) for i in range(lax.axis_size(axis))])


def from_tp(value, shift):
    if shift == 0:
        return value
    size = lax.axis_size("tp")
    return lax.ppermute(value, "tp", [(i, (i + shift) % size) for i in range(size)])


def rotate(values, places):
    inverse = 1.0 / ROPE_BASE ** (jnp.arange(0, HD, 2).astype(jnp.float32) / HD)
    angles = places.astype(jnp.float32)[:, None] * inverse[None, :]
    cosine = jnp.concatenate([jnp.cos(angles), jnp.cos(angles)], axis=-1)[:, None, :]
    sine = jnp.concatenate([jnp.sin(angles), jnp.sin(angles)], axis=-1)[:, None, :]
    first_half = values[..., : HD // 2]
    second_half = values[..., HD // 2 :]
    turned = jnp.concatenate([-second_half, first_half], axis=-1)
    return values * cosine + turned * sine


def absorb(state, queries, block_keys, block_values, allowed, scale):
    running_max, running_sum, output = state
    scores = (
        jnp.einsum("qcgd,kcd->cgqk", queries, block_keys, preferred_element_type=jnp.float32)
        * scale
    )
    scores = jnp.where(allowed[None, None], scores, FLOOR_SCORE)
    new_max = jnp.maximum(running_max, jnp.max(scores, axis=-1))
    factor = jnp.exp(running_max - new_max)
    weights = jnp.where(allowed[None, None], jnp.exp(scores - new_max[..., None]), 0.0)
    running_sum = running_sum * factor + jnp.sum(weights, axis=-1)
    mixed = jnp.einsum(
        "cgqk,kcd->qcgd",
        weights.astype(jnp.bfloat16),
        block_values,
        preferred_element_type=jnp.float32,
    )
    output = output * jnp.transpose(factor, (2, 0, 1))[..., None] + mixed
    return (new_max, running_sum, output)


def output_rows(w_out):
    parts = lax.axis_size("tp")
    rows, width = w_out.shape
    share = rows // parts
    pieces = lax.all_to_all(w_out.reshape(parts, share, width), "tp", 0, 0, tiled=True)
    mine = jnp.transpose(pieces, (1, 0, 2)).reshape(share, parts * width)
    padded = -(-share // 8) * 8
    mine = jnp.pad(mine, ((0, padded - share), (0, 0)))
    return (lax.all_gather(mine, "req", axis=0, tiled=True), share)


def shards(q_new, k_new, v_new, k_cache, v_cache, lengths, page_table, w_out):
    own_rows = q_new.shape[0]
    all_rows = 2 * own_rows
    local_heads = k_new.shape[1] // HD
    pages_local = k_cache.shape[0]
    page_rows = k_cache.shape[1]
    block_rows = BLOCK_PAGES * page_rows
    scale = 1.0 / math.sqrt(HD)
    weights_mine, share = output_rows(w_out)
    device_row = lax.axis_index("req")
    parity = device_row % 2
    request = device_row // 2
    length = lengths[request]
    own_places = length + parity * own_rows + jnp.arange(own_rows)
    own_queries = rotate(
        q_new.reshape(own_rows, local_heads * GROUP, HD).astype(jnp.float32), own_places
    ).astype(jnp.bfloat16)
    own_keys = rotate(
        k_new.reshape(own_rows, local_heads, HD).astype(jnp.float32), own_places
    ).astype(jnp.bfloat16)
    own_values = v_new.reshape(own_rows, local_heads, HD)
    peer_queries, peer_keys, peer_values = from_partner(
        (own_queries, own_keys, own_values), "req", 0
    )

    def ordered(mine, theirs):
        return jnp.where(
            parity == 0,
            jnp.concatenate([mine, theirs], axis=0),
            jnp.concatenate([theirs, mine], axis=0),
        )

    queries = ordered(own_queries, peer_queries).reshape(all_rows, local_heads, GROUP, HD)
    fresh_keys = ordered(own_keys, peer_keys)
    fresh_values = ordered(own_values, peer_values)
    state = (
        jnp.full((local_heads, GROUP, all_rows), FLOOR_SCORE, jnp.float32),
        jnp.zeros((local_heads, GROUP, all_rows), jnp.float32),
        jnp.zeros((all_rows, local_heads, GROUP, HD), jnp.float32),
    )
    token_index = jnp.arange(all_rows)
    causal = (token_index[None, :] <= token_index[:, None]) & (parity == 1)
    state = absorb(state, queries, fresh_keys, fresh_values, causal, scale)
    page_count = (length + page_rows - 1) // page_rows
    even_pages = (page_count + 1) // 2
    first_page = jnp.where(parity == 0, 0, even_pages)
    last_page = jnp.where(parity == 0, even_pages, page_count)
    table_row = jnp.concatenate([page_table[request], jnp.full((BLOCK_PAGES,), -1, jnp.int32)])
    offset = device_row * pages_local
    block_count = (last_page - first_page + BLOCK_PAGES - 1) // BLOCK_PAGES

    def visit(block, carry):
        block_first = first_page + block * BLOCK_PAGES
        logical = block_first + jnp.arange(BLOCK_PAGES)
        physical = lax.dynamic_slice(table_row, (block_first,), (BLOCK_PAGES,))
        slots = jnp.clip(physical - offset, 0, pages_local - 1)
        block_keys = k_cache[slots].reshape(block_rows, local_heads, HD)
        block_values = v_cache[slots].reshape(block_rows, local_heads, HD)
        key_places = (logical[:, None] * page_rows + jnp.arange(page_rows)[None, :]).reshape(
            block_rows
        )
        usable = jnp.repeat(logical < last_page, page_rows) & (key_places < length)
        allowed = jnp.broadcast_to(usable[None, :], (all_rows, block_rows))
        return absorb(carry, queries, block_keys, block_values, allowed, scale)

    running_max, running_sum, output = lax.fori_loop(0, block_count, visit, state)
    peer_start = (1 - parity) * own_rows
    own_start = parity * own_rows
    outgoing = (
        lax.dynamic_slice_in_dim(output, peer_start, own_rows, 0),
        lax.dynamic_slice_in_dim(running_max, peer_start, own_rows, 2),
        lax.dynamic_slice_in_dim(running_sum, peer_start, own_rows, 2),
    )
    other_output, other_max, other_sum = (
        from_partner(outgoing[0].astype(jnp.bfloat16), "req", 0).astype(jnp.float32),
        from_partner(outgoing[1].astype(jnp.bfloat16), "req", 0).astype(jnp.float32),
        from_partner(outgoing[2].astype(jnp.bfloat16), "req", 0).astype(jnp.float32),
    )
    mine_output = lax.dynamic_slice_in_dim(output, own_start, own_rows, 0)
    mine_max = lax.dynamic_slice_in_dim(running_max, own_start, own_rows, 2)
    mine_sum = lax.dynamic_slice_in_dim(running_sum, own_start, own_rows, 2)
    joint_max = jnp.maximum(mine_max, other_max)
    mine_factor = jnp.exp(mine_max - joint_max)
    other_factor = jnp.exp(other_max - joint_max)
    joint_sum = mine_sum * mine_factor + other_sum * other_factor
    joint_output = (
        mine_output * jnp.transpose(mine_factor, (2, 0, 1))[..., None]
        + other_output * jnp.transpose(other_factor, (2, 0, 1))[..., None]
    )
    attention = (
        (joint_output / jnp.transpose(joint_sum, (2, 0, 1))[..., None])
        .reshape(own_rows, local_heads * GROUP * HD)
        .astype(jnp.bfloat16)
    )
    parts = lax.axis_size("tp")
    full_rows = lax.all_gather(attention, "tp", axis=1, tiled=True)
    projected = lax.dot_general(
        full_rows, weights_mine, (((1,), (1,)), ((), ())), preferred_element_type=jnp.float32
    )
    blocks = weights_mine.shape[0] // (-(-share // 8) * 8)
    projected = projected.reshape(own_rows, blocks, -1)[:, :, :share].astype(jnp.bfloat16)
    gathered = jnp.stack([from_tp(projected, shift) for shift in range(parts)])
    sources = (lax.axis_index("tp") - jnp.arange(parts)) % parts
    gathered = jnp.take(gathered, sources, axis=0)
    return jnp.transpose(gathered, (1, 2, 0, 3)).reshape(own_rows, -1)


def solution(mesh):
    in_specs = (
        P("req", "tp"),
        P("req", "tp"),
        P("req", "tp"),
        P("req", None, "tp"),
        P("req", None, "tp"),
        P(),
        P(),
        P("req", "tp"),
    )
    out_specs = P("req", None)
    return jax.shard_map(shards, mesh=mesh, in_specs=in_specs, out_specs=out_specs, check_vma=False)
```

profile of v0, /device:TPU:9, one launch (start us, length us, event | category | flops | bytes accessed | tf_op | source)
XLA Modules:
  0.0 202.3 jit_solution(11156302024861886297)
XLA Ops:
  7.5 13.9 %all_to_all.5 = bf16[8,10,640]{2,1,0:T(8,128)(2,1)S(1)} all-to-all(bf16[8,10,640]{2,1,0:T(8,128)(2,1)S(1)} %reshape.364), channel_id=1, replica_groups=mesh['req'=64,'tp'=8] {'tp'}, dimensions={0} | all-to-all | bytes 204800 | tf_op jit(solution)/shard_map/all_to_all | solution.py:61
  25.1 4.9 %collective-permute-start.1 = (bf16[64,5,128]{2,1,0:T(8,128)(2,1)S(1)}, bf16[64,5,128]{2,1,0:T(8,128)(2,1)S(1)}, u32[]{:S(2)}, u32[]{:S(2)}) collective-permute-start(bf16[64,5,128]{2,1,0:T(8,128)(2,1)S(1)} %fusion.25), channel_id=1, source_target_pairs={{0,8},{8,0},{16,24},{24,16},{32,40},{40,32},{48,56},{56,48},{64,72... | collective-permute-start | bytes 245768 | tf_op jit(solution)/shard_map/ppermute | solution.py:15
  30.0 1.9 collective-permute-start
  31.9 2.4 %collective-permute-start.2 = (bf16[64,1,128]{2,0,1:T(8,128)(2,1)S(1)}, bf16[64,1,128]{2,0,1:T(8,128)(2,1)S(1)}, u32[]{:S(2)}, u32[]{:S(2)}) collective-permute-start(bf16[64,1,128]{2,0,1:T(8,128)(2,1)S(1)} %bitcast.190), channel_id=1, source_target_pairs={{0,8},{8,0},{16,24},{24,16},{32,40},{40,32},{48,56},{56,48},{64,72... | collective-permute-start | bytes 49160 | tf_op jit(solution)/shard_map/ppermute | solution.py:15
  36.0 20.8 %while.14 = (s32[]{:T(128)}, f32[1,5,128]{2,1,0:T(8,128)S(1)}, f32[1,5,128]{2,1,0:T(8,128)S(1)}, f32[128,1,5,128]{0,3,2,1:T(8,128)S(1)}, s32[]{:T(128)}, /*index...) while((s32[]{:T(128)}, f32[1,5,128]{2,1,0:T(8,128)S(1)}, ...), condition=%wide.region_5.6_spmd, body=%wide.region_2.5_spmd.sunk | while | flops 170889632 | bytes 5585255 | solution.py:133
  36.1 1.6 gather_fusion
  38.8 1.6 gather_fusion.1
  41.3 1.6 gather_fusion
  44.0 1.6 gather_fusion.1
  46.5 1.6 gather_fusion
  49.2 1.6 gather_fusion.1
  51.7 1.6 gather_fusion
  54.3 1.6 gather_fusion.1
  56.8 1.9 collective-permute-start.3
  58.9 2.4 %collective-permute-start.5 = (bf16[1,5,64]{2,1,0:T(8,128)(2,1)S(1)}, bf16[1,5,64]{2,1,0:T(8,128)(2,1)S(1)}, u32[]{:S(2)}, u32[]{:S(2)}) collective-permute-start(bf16[1,5,64]{2,1,0:T(8,128)(2,1)S(1)} %dynamic-slice_convert_fusion.1), channel_id=1, source_target_pairs={{0,8},{8,0},{16,24},{24,16},{32,40},{40,32},{48,56},{56,48},{64,72... | collective-permute-start | bytes 1928 | tf_op jit(solution)/shard_map/ppermute | solution.py:15
  61.4 1.9 collective-permute-start.4
  64.8 22.3 %all_gather.6 = bf16[64,5120]{0,1:T(8,128)(2,1)S(1)} all-gather(bf16[64,640]{0,1:T(8,128)(2,1)S(1)} %bitcast.187), channel_id=1, replica_groups=mesh['req'=64,'tp'=8] {'tp'}, dimensions={1}, use_global_device_ids=true | all-gather | bytes 737280 | tf_op jit(solution)/shard_map/all_gather | solution.py:163
  87.1 29.9 %all-gather.2.cloned.1.call-done = bf16[1024,5120]{1,0:T(8,128)(2,1)} async-done(((bf16[16,5120]{1,0:T(8,128)(2,1)}), bf16[1024,5120]{1,0:T(8,128)(2,1)}) %all-gather.2.cloned.1.call-update) | async-done | bytes 10485776 | tf_op jit(solution)/shard_map/all_gather | solution.py:65
  117.0 7.3 %convolution_convert_fusion = bf16[64,1024]{1,0:T(8,128)(2,1)S(1)} fusion(bf16[64,5120]{0,1:T(8,128)(2,1)S(1)} %all_gather.6, bf16[1024,5120]{1,0:T(8,128)(2,1)} %all-gather.2.cloned.1.call-done), kind=kOutput, calls=%fused_computation.37 | convolution fusion | flops 671154176 | bytes 11272192 | tf_op jit(solution)/shard_map/dot_general | solution.py:164
  124.5 3.1 %collective-permute-start.6 = (bf16[64,64,10]{0,2,1:T(8,128)(2,1)S(1)}, bf16[64,64,10]{0,2,1:T(8,128)(2,1)S(1)}, u32[]{:S(2)}, u32[]{:S(2)}) collective-permute-start(bf16[64,64,10]{0,2,1:T(8,128)(2,1)S(1)} %bitcast.176), channel_id=1, source_target_pairs={{0,1},{1,2},{2,3},{3,4},{4,5},{5,6},{6,7},{7,0},{8,9},{9,10},{10,1... | collective-permute-start | bytes 245768 | tf_op jit(solution)/shard_map/ppermute | solution.py:22
  128.3 5.2 %collective-permute-start.7 = (bf16[64,64,10]{0,2,1:T(8,128)(2,1)S(1)}, bf16[64,64,10]{0,2,1:T(8,128)(2,1)S(1)}, u32[]{:S(2)}, u32[]{:S(2)}) collective-permute-start(bf16[64,64,10]{0,2,1:T(8,128)(2,1)S(1)} %bitcast.178), channel_id=1, source_target_pairs={{0,2},{1,3},{2,4},{3,5},{4,6},{5,7},{6,0},{7,1},{8,10},{9,11},{10,... | collective-permute-start | bytes 245768 | tf_op jit(solution)/shard_map/ppermute | solution.py:22
  133.6 2.3 %collective-permute-start.8 = (bf16[64,64,10]{0,2,1:T(8,128)(2,1)S(1)}, bf16[64,64,10]{0,2,1:T(8,128)(2,1)S(1)}, u32[]{:S(2)}, u32[]{:S(2)}) collective-permute-start(bf16[64,64,10]{0,2,1:T(8,128)(2,1)S(1)} %bitcast.179), channel_id=1, source_target_pairs={{0,3},{1,4},{2,5},{3,6},{4,7},{5,0},{6,1},{7,2},{8,11},{9,12},{10,... | collective-permute-start | bytes 245768 | tf_op jit(solution)/shard_map/ppermute | solution.py:22
  135.8 4.8 %collective-permute-start.9 = (bf16[64,64,10]{0,2,1:T(8,128)(2,1)S(1)}, bf16[64,64,10]{0,2,1:T(8,128)(2,1)S(1)}, u32[]{:S(2)}, u32[]{:S(2)}) collective-permute-start(bf16[64,64,10]{0,2,1:T(8,128)(2,1)S(1)} %bitcast.180), channel_id=1, source_target_pairs={{0,4},{1,5},{2,6},{3,7},{4,0},{5,1},{6,2},{7,3},{8,12},{9,13},{10,... | collective-permute-start | bytes 245768 | tf_op jit(solution)/shard_map/ppermute | solution.py:22
  140.6 3.3 %collective-permute-start.10 = (bf16[64,64,10]{0,2,1:T(8,128)(2,1)S(1)}, bf16[64,64,10]{0,2,1:T(8,128)(2,1)S(1)}, u32[]{:S(2)}, u32[]{:S(2)}) collective-permute-start(bf16[64,64,10]{0,2,1:T(8,128)(2,1)S(1)} %bitcast.181), channel_id=1, source_target_pairs={{0,5},{1,6},{2,7},{3,0},{4,1},{5,2},{6,3},{7,4},{8,13},{9,14},{10,... | collective-permute-start | bytes 245768 | tf_op jit(solution)/shard_map/ppermute | solution.py:22
  144.0 4.1 %collective-permute-start.11 = (bf16[64,64,10]{0,2,1:T(8,128)(2,1)S(1)}, bf16[64,64,10]{0,2,1:T(8,128)(2,1)S(1)}, u32[]{:S(2)}, u32[]{:S(2)}) collective-permute-start(bf16[64,64,10]{0,2,1:T(8,128)(2,1)S(1)} %bitcast.182), channel_id=1, source_target_pairs={{0,6},{1,7},{2,0},{3,1},{4,2},{5,3},{6,4},{7,5},{8,14},{9,15},{10,... | collective-permute-start | bytes 245768 | tf_op jit(solution)/shard_map/ppermute | solution.py:22
  148.8 4.3 %collective-permute-start.12 = (bf16[64,64,10]{0,2,1:T(8,128)(2,1)S(1)}, bf16[64,64,10]{0,2,1:T(8,128)(2,1)S(1)}, u32[]{:S(2)}, u32[]{:S(2)}) collective-permute-start(bf16[64,64,10]{0,2,1:T(8,128)(2,1)S(1)} %bitcast.183), channel_id=1, source_target_pairs={{0,7},{1,0},{2,1},{3,2},{4,3},{5,4},{6,5},{7,6},{8,15},{9,8},{10,9... | collective-permute-start | bytes 245768 | tf_op jit(solution)/shard_map/ppermute | solution.py:22
  153.8 8.7 %collective-permute-done.8 = bf16[64,64,10]{0,2,1:T(8,128)(2,1)S(1)} collective-permute-done((bf16[64,64,10]{0,2,1:T(8,128)(2,1)S(1)}, bf16[64,64,10]{0,2,1:T(8,128)(2,1)S(1)}, u32[]{:S(2)}, u32[]{:S(2)}) %collective-permute-start.8) | collective-permute-done | bytes 81952 | tf_op jit(solution)/shard_map/ppermute | solution.py:22
  164.0 9.0 %collective-permute-done.10 = bf16[64,64,10]{0,2,1:T(8,128)(2,1)S(1)} collective-permute-done((bf16[64,64,10]{0,2,1:T(8,128)(2,1)S(1)}, bf16[64,64,10]{0,2,1:T(8,128)(2,1)S(1)}, u32[]{:S(2)}, u32[]{:S(2)}) %collective-permute-start.10) | collective-permute-done | bytes 81952 | tf_op jit(solution)/shard_map/ppermute | solution.py:22
  173.8 4.1 %collective-permute-done.11 = bf16[64,64,10]{0,2,1:T(8,128)(2,1)S(1)} collective-permute-done((bf16[64,64,10]{0,2,1:T(8,128)(2,1)S(1)}, bf16[64,64,10]{0,2,1:T(8,128)(2,1)S(1)}, u32[]{:S(2)}, u32[]{:S(2)}) %collective-permute-start.11) | collective-permute-done | bytes 81952 | tf_op jit(solution)/shard_map/ppermute | solution.py:22
  178.6 10.6 %collective-permute-done.12 = bf16[64,64,10]{0,2,1:T(8,128)(2,1)S(1)} collective-permute-done((bf16[64,64,10]{0,2,1:T(8,128)(2,1)S(1)}, bf16[64,64,10]{0,2,1:T(8,128)(2,1)S(1)}, u32[]{:S(2)}, u32[]{:S(2)}) %collective-permute-start.12) | collective-permute-done | bytes 81952 | tf_op jit(solution)/shard_map/ppermute | solution.py:22
  189.9 2.5 %gather_fusion.2 = bf16[8,64,64,10]{1,3,2,0:T(8,128)(2,1)S(1)} fusion(bf16[8,64,64,10]{1,3,2,0:T(8,128)(2,1)} %bitcast_dynamic-update-slice_fusion, s32[1024]{0:T(1024)S(1)} %pad_clamp_fusion.1), kind=kCustom, calls=%fused_computation.2 | custom fusion | bytes 1310752 | tf_op jit(solution)/shard_map/jit(_take)/gather | solution.py:171
  194.1 1.3 copy.23
  (109 shorter events, 21.6 us)
Async XLA Ops:
  6.5 28.4 %copy-start = (s32[32,32]{1,0:T(8,128)S(1)}, s32[32,32]{1,0:T(8,128)}, u32[]{:S(2)}) copy-start(s32[32,32]{1,0:T(8,128)} %param.16) | copy-start | bytes 12292
  6.5 16.7 %copy-start.3 = (s32[32]{0:T(128)S(1)}, s32[32]{0:T(128)}, u32[]{:S(2)}) copy-start(s32[32]{0:T(128)} %param.15) | copy-start | bytes 388
  6.5 17.9 %copy-start.1 = (bf16[64,128]{1,0:T(8,128)(2,1)S(1)}, bf16[64,128]{1,0:T(8,128)(2,1)}, u32[]{:S(2)}) copy-start(bf16[64,128]{1,0:T(8,128)(2,1)} %param.11) | copy-start | bytes 49156
  6.5 110.5 %all-gather.2.cloned.1.call-start = ((), (), s32[]{:S(2)}) async-start(), calls=%async_computation.1 | async-start | bytes 10649600 | tf_op jit(solution)/shard_map/all_gather | solution.py:65
  21.4 10.5 %copy-start.2 = (bf16[64,128]{1,0:T(8,128)(2,1)S(1)}, bf16[64,128]{1,0:T(8,128)(2,1)}, u32[]{:S(2)}) copy-start(bf16[64,128]{1,0:T(8,128)(2,1)} %param.12) | copy-start | bytes 49156
  25.1 10.0 %collective-permute-start.1 = (bf16[64,5,128]{2,1,0:T(8,128)(2,1)S(1)}, bf16[64,5,128]{2,1,0:T(8,128)(2,1)S(1)}, u32[]{:S(2)}, u32[]{:S(2)}) collective-permute-start(bf16[64,5,128]{2,1,0:T(8,128)(2,1)S(1)} %fusion.25), channel_id=1, source_target_pairs={{0,8},{8,0},{16,24},{24,16},{32,40},{40,32},{48,56},{56,48},{64,72... | collective-permute-start | bytes 245768 | tf_op jit(solution)/shard_map/ppermute | solution.py:15
  30.0 5.3 %collective-permute-start = (bf16[64,1,128]{2,0,1:T(8,128)(2,1)S(1)}, bf16[64,1,128]{2,0,1:T(8,128)(2,1)S(1)}, u32[]{:S(2)}, u32[]{:S(2)}) collective-permute-start(bf16[64,1,128]{2,0,1:T(8,128)(2,1)S(1)} %bitcast.189), channel_id=1, source_target_pairs={{0,8},{8,0},{16,24},{24,16},{32,40},{40,32},{48,56},{56,48},{64,72... | collective-permute-start | bytes 49160 | tf_op jit(solution)/shard_map/ppermute | solution.py:15
  31.9 3.8 %collective-permute-start.2 = (bf16[64,1,128]{2,0,1:T(8,128)(2,1)S(1)}, bf16[64,1,128]{2,0,1:T(8,128)(2,1)S(1)}, u32[]{:S(2)}, u32[]{:S(2)}) collective-permute-start(bf16[64,1,128]{2,0,1:T(8,128)(2,1)S(1)} %bitcast.190), channel_id=1, source_target_pairs={{0,8},{8,0},{16,24},{24,16},{32,40},{40,32},{48,56},{56,48},{64,72... | collective-permute-start | bytes 49160 | tf_op jit(solution)/shard_map/ppermute | solution.py:15
  56.8 6.5 %collective-permute-start.3 = (bf16[1,5,64]{2,1,0:T(8,128)(2,1)S(1)}, bf16[1,5,64]{2,1,0:T(8,128)(2,1)S(1)}, u32[]{:S(2)}, u32[]{:S(2)}) collective-permute-start(bf16[1,5,64]{2,1,0:T(8,128)(2,1)S(1)} %dynamic-slice_convert_fusion.2), channel_id=1, source_target_pairs={{0,8},{8,0},{16,24},{24,16},{32,40},{40,32},{48,56},{56,48},{64,72... | collective-permute-start | bytes 1928 | tf_op jit(solution)/shard_map/ppermute | solution.py:15
  58.9 4.5 %collective-permute-start.5 = (bf16[1,5,64]{2,1,0:T(8,128)(2,1)S(1)}, bf16[1,5,64]{2,1,0:T(8,128)(2,1)S(1)}, u32[]{:S(2)}, u32[]{:S(2)}) collective-permute-start(bf16[1,5,64]{2,1,0:T(8,128)(2,1)S(1)} %dynamic-slice_convert_fusion.1), channel_id=1, source_target_pairs={{0,8},{8,0},{16,24},{24,16},{32,40},{40,32},{48,56},{56,48},{64,72... | collective-permute-start | bytes 1928 | tf_op jit(solution)/shard_map/ppermute | solution.py:15
  61.4 3.3 %collective-permute-start.4 = (bf16[64,1,5,128]{0,3,2,1:T(8,128)(2,1)S(1)}, bf16[64,1,5,128]{0,3,2,1:T(8,128)(2,1)S(1)}, u32[]{:S(2)}, u32[]{:S(2)}) collective-permute-start(bf16[64,1,5,128]{0,3,2,1:T(8,128)(2,1)S(1)} %dynamic-slice_convert_fusion), channel_id=1, source_target_pairs={{0,8},{8,0},{16,24},{24,16},{32,40},{40,32},{48,56},{56,48},{64,72... | collective-permute-start | bytes 245768 | tf_op jit(solution)/shard_map/ppermute | solution.py:15
  124.5 19.5 %collective-permute-start.6 = (bf16[64,64,10]{0,2,1:T(8,128)(2,1)S(1)}, bf16[64,64,10]{0,2,1:T(8,128)(2,1)S(1)}, u32[]{:S(2)}, u32[]{:S(2)}) collective-permute-start(bf16[64,64,10]{0,2,1:T(8,128)(2,1)S(1)} %bitcast.176), channel_id=1, source_target_pairs={{0,1},{1,2},{2,3},{3,4},{4,5},{5,6},{6,7},{7,0},{8,9},{9,10},{10,1... | collective-permute-start | bytes 245768 | tf_op jit(solution)/shard_map/ppermute | solution.py:22
  128.3 20.5 %collective-permute-start.7 = (bf16[64,64,10]{0,2,1:T(8,128)(2,1)S(1)}, bf16[64,64,10]{0,2,1:T(8,128)(2,1)S(1)}, u32[]{:S(2)}, u32[]{:S(2)}) collective-permute-start(bf16[64,64,10]{0,2,1:T(8,128)(2,1)S(1)} %bitcast.178), channel_id=1, source_target_pairs={{0,2},{1,3},{2,4},{3,5},{4,6},{5,7},{6,0},{7,1},{8,10},{9,11},{10,... | collective-permute-start | bytes 245768 | tf_op jit(solution)/shard_map/ppermute | solution.py:22
  133.6 29.0 %collective-permute-start.8 = (bf16[64,64,10]{0,2,1:T(8,128)(2,1)S(1)}, bf16[64,64,10]{0,2,1:T(8,128)(2,1)S(1)}, u32[]{:S(2)}, u32[]{:S(2)}) collective-permute-start(bf16[64,64,10]{0,2,1:T(8,128)(2,1)S(1)} %bitcast.179), channel_id=1, source_target_pairs={{0,3},{1,4},{2,5},{3,6},{4,7},{5,0},{6,1},{7,2},{8,11},{9,12},{10,... | collective-permute-start | bytes 245768 | tf_op jit(solution)/shard_map/ppermute | solution.py:22
  135.8 27.4 %collective-permute-start.9 = (bf16[64,64,10]{0,2,1:T(8,128)(2,1)S(1)}, bf16[64,64,10]{0,2,1:T(8,128)(2,1)S(1)}, u32[]{:S(2)}, u32[]{:S(2)}) collective-permute-start(bf16[64,64,10]{0,2,1:T(8,128)(2,1)S(1)} %bitcast.180), channel_id=1, source_target_pairs={{0,4},{1,5},{2,6},{3,7},{4,0},{5,1},{6,2},{7,3},{8,12},{9,13},{10,... | collective-permute-start | bytes 245768 | tf_op jit(solution)/shard_map/ppermute | solution.py:22
  140.6 32.4 %collective-permute-start.10 = (bf16[64,64,10]{0,2,1:T(8,128)(2,1)S(1)}, bf16[64,64,10]{0,2,1:T(8,128)(2,1)S(1)}, u32[]{:S(2)}, u32[]{:S(2)}) collective-permute-start(bf16[64,64,10]{0,2,1:T(8,128)(2,1)S(1)} %bitcast.181), channel_id=1, source_target_pairs={{0,5},{1,6},{2,7},{3,0},{4,1},{5,2},{6,3},{7,4},{8,13},{9,14},{10,... | collective-permute-start | bytes 245768 | tf_op jit(solution)/shard_map/ppermute | solution.py:22
  144.0 33.9 %collective-permute-start.11 = (bf16[64,64,10]{0,2,1:T(8,128)(2,1)S(1)}, bf16[64,64,10]{0,2,1:T(8,128)(2,1)S(1)}, u32[]{:S(2)}, u32[]{:S(2)}) collective-permute-start(bf16[64,64,10]{0,2,1:T(8,128)(2,1)S(1)} %bitcast.182), channel_id=1, source_target_pairs={{0,6},{1,7},{2,0},{3,1},{4,2},{5,3},{6,4},{7,5},{8,14},{9,15},{10,... | collective-permute-start | bytes 245768 | tf_op jit(solution)/shard_map/ppermute | solution.py:22
  148.8 40.3 %collective-permute-start.12 = (bf16[64,64,10]{0,2,1:T(8,128)(2,1)S(1)}, bf16[64,64,10]{0,2,1:T(8,128)(2,1)S(1)}, u32[]{:S(2)}, u32[]{:S(2)}) collective-permute-start(bf16[64,64,10]{0,2,1:T(8,128)(2,1)S(1)} %bitcast.183), channel_id=1, source_target_pairs={{0,7},{1,0},{2,1},{3,2},{4,3},{5,4},{6,5},{7,6},{8,15},{9,8},{10,9... | collective-permute-start | bytes 245768 | tf_op jit(solution)/shard_map/ppermute | solution.py:22
Sparse Core Ops, SparseCore 0:
  22.3 94.6 all-gather.1
where the time goes:
time: 203 us; the launch traced here: 202 us
  waiting for transfers between devices  63.6 us (31%)
  starting transfers between devices  42.6 us (21%)
  blocking collectives  36.2 us (18%)
  local copies, waits for them, and re-layouts  27.7 us (14%)
  between operations  15.1 us (7%)
  matrix products  11.1 us (5%)
  other arithmetic  5.6 us (3%)
    ppermute x7, waiting for transfers between devices, from_tp(): lax.ppermute(value, 'tp', [(i, (i + shift) % size) for i in range(size)])  32.5 us
    all_gather x1, waiting for transfers between devices, output_rows(): return (lax.all_gather(mine, 'req', axis=0, tiled=True), share)  29.9 us
    ppermute x7, starting transfers between devices, from_tp(): lax.ppermute(value, 'tp', [(i, (i + shift) % size) for i in range(size)])  27.1 us
    all_gather x1, blocking collectives, shards(): full_rows = lax.all_gather(attention, 'tp', axis=1, tiled=True)  22.3 us
    ppermute x6, starting transfers between devices, from_partner(): lax.ppermute(value, axis, [(i, i ^ 1 << distance) for i in range(lax.axis...  15.4 us
    all_to_all x1, blocking collectives, output_rows(): lax.all_to_all(w_out.reshape(parts, share, width), 'tp', 0, 0, tiled=True)  13.9 us
    dot_general x1, matrix products, shards(): lax.dot_general(full_rows, weights_mine, (((1,), (1,)), ((), ())), prefer...  7.29 us
    gather x4, local copies, waits for them, and re-layouts, visit(): block_values = v_cache[slots].reshape(block_rows, local_heads, HD)  6.49 us
  transfers between devices with their start and end apart: 14, of which 6 were waited for; matrix products, arithmetic and copies ran while one was open for 14% of the time, Pallas kernels for 0%

commit v1 on v0

--- a/solution.py
+++ b/solution.py
@@ -62,7 +62,16 @@
     mine = jnp.transpose(pieces, (1, 0, 2)).reshape(share, parts * width)
     padded = -(-share // 8) * 8
     mine = jnp.pad(mine, ((0, padded - share), (0, 0)))
-    return (lax.all_gather(mine, "req", axis=0, tiled=True), share)
+    unite_joints_on = lambda in_array, shard_axis, row_dim: jnp.concatenate(
+        lax.all_to_all(
+            jnp.stack(lax.axis_size(shard_axis) * [in_array], 0),
+            split_axis=0,
+            concat_axis=0,
+            axis_name=shard_axis,
+        ),
+        axis=row_dim,
+    )
+    return (unite_joints_on(mine, "req", 0), share)
 
 
 def shards(q_new, k_new, v_new, k_cache, v_cache, lengths, page_table, w_out):

time: 203 us -> 338 us (1.67)
  the two profiles are of different devices: /device:TPU:9 before, /device:TPU:69 now
where the time goes in v1:
time: 338 us; the launch traced here: 337 us
  waiting for transfers between devices  198 us (59%)
  starting transfers between devices  51.8 us (15%)
  blocking collectives  36.9 us (11%)
  local copies, waits for them, and re-layouts  23.6 us (7%)
  matrix products  18.8 us (6%)
  other arithmetic  5.81 us (2%)
    all_to_all x1, waiting for transfers between devices, output_rows(): lax.all_to_all(jnp.stack(lax.axis_size(shard_axis) * [in_array], 0), spli...  176 us
    ppermute x7, starting transfers between devices, from_tp(): lax.ppermute(value, 'tp', [(i, (i + shift) % size) for i in range(size)])  23.4 us
    all_gather x1, blocking collectives, shards(): full_rows = lax.all_gather(attention, 'tp', axis=1, tiled=True)  22.2 us
    ppermute x7, waiting for transfers between devices, from_tp(): lax.ppermute(value, 'tp', [(i, (i + shift) % size) for i in range(size)])  20.2 us
    dot_general x1, matrix products, shards(): lax.dot_general(full_rows, weights_mine, (((1,), (1,)), ((), ())), prefer...  15.8 us
    all_to_all x1, starting transfers between devices, output_rows(): lax.all_to_all(jnp.stack(lax.axis_size(shard_axis) * [in_array], 0), spli...  15.4 us
    all_to_all x1, blocking collectives, output_rows(): lax.all_to_all(w_out.reshape(parts, share, width), 'tp', 0, 0, tiled=True)  14.8 us
    ppermute x6, starting transfers between devices, from_partner(): lax.ppermute(value, axis, [(i, i ^ 1 << distance) for i in range(lax.axis...  13 us
  transfers between devices with their start and end apart: 14, of which 7 were waited for; matrix products, arithmetic and copies ran while one was open for 5% of the time, Pallas kernels for 0%

profile of v1, /device:TPU:69, one launch (start us, length us, event | category | flops | bytes accessed | tf_op | source)
XLA Modules:
  0.0 336.7 jit_solution(9405914986650372419)
XLA Ops:
  1.0 14.8 %all_to_all.10 = bf16[8,10,640]{2,1,0:T(8,128)(2,1)S(1)} all-to-all(bf16[8,10,640]{2,1,0:T(8,128)(2,1)S(1)} %reshape.366), channel_id=1, replica_groups=mesh['req'=64,'tp'=8] {'tp'}, dimensions={0} | all-to-all | bytes 204800 | tf_op jit(solution)/shard_map/all_to_all | solution.py:61
  15.8 5.1 %stack.20 = bf16[64,16,5120]{2,1,0:T(8,128)(2,1)} broadcast(bf16[16,5120]{1,0:T(8,128)(2,1)S(1)} %pad.5), dimensions={1,2} | broadcast | bytes 10649600 | tf_op jit(solution)/shard_map/stack | solution.py:67
  21.0 15.4 %all-to-all-start.1 = ((bf16[64,16,5120]{2,1,0:T(8,128)(2,1)}), bf16[64,16,5120]{2,1,0:T(8,128)(2,1)}, u32[]{:S(2)}, u32[]{:S(2)}) async-start(bf16[64,16,5120]{2,1,0:T(8,128)(2,1)} %stack.20), calls=%async_computation.1 | async-start | bytes 20971520 | tf_op jit(solution)/shard_map/all_to_all | solution.py:66
  38.6 2.3 collective-permute-start.1
  40.9 2.1 collective-permute-start
  42.9 2.3 collective-permute-start.2
  46.9 15.8 %while.14 = (s32[]{:T(128)}, f32[1,5,128]{2,1,0:T(8,128)S(1)}, f32[1,5,128]{2,1,0:T(8,128)S(1)}, f32[128,1,5,128]{0,3,2,1:T(8,128)S(1)}, s32[]{:T(128)}, /*index...) while((s32[]{:T(128)}, f32[1,5,128]{2,1,0:T(8,128)S(1)}, ...), condition=%wide.region_5.6_spmd, body=%wide.region_2.5_spmd.sunk | while | flops 170889632 | bytes 5585263 | solution.py:142
  47.0 1.6 gather_fusion
  50.1 1.6 gather_fusion.1
  52.3 1.6 gather_fusion
  55.3 1.6 gather_fusion.1
  57.5 1.6 gather_fusion
  60.6 1.6 gather_fusion.1
  62.8 2.0 collective-permute-start.3
  64.9 2.3 collective-permute-start.5
  67.3 2.1 collective-permute-start.4
  70.9 22.2 %all_gather.3 = bf16[64,5120]{1,0:T(8,128)(2,1)S(1)} all-gather(bf16[64,640]{1,0:T(8,128)(2,1)S(1)} %copy.51), channel_id=1, replica_groups=mesh['req'=64,'tp'=8] {'tp'}, dimensions={1}, use_global_device_ids=true | all-gather | bytes 737280 | tf_op jit(solution)/shard_map/all_gather | solution.py:172
  93.0 176.2 %all-to-all-done.1 = bf16[64,16,5120]{2,1,0:T(8,128)(2,1)} async-done(((bf16[64,16,5120]{2,1,0:T(8,128)(2,1)}), bf16[64,16,5120]{2,1,0:T(8,128)(2,1)}, u32[]{:S(2)}, u32[]{:S(2)}) %all-to-all-start.1) | async-done | bytes 10485792 | tf_op jit(solution)/shard_map/all_to_all | solution.py:66
  269.3 15.8 %fusion.19 = bf16[64,64,16]{1,0,2:T(8,128)(2,1)S(1)} fusion(bf16[64,16,5120]{2,1,0:T(8,128)(2,1)} %all-to-all-done.1, bf16[64,5120]{1,0:T(8,128)(2,1)S(1)} %all_gather.3), kind=kOutput, calls=%fused_computation.32 | convolution fusion | flops 671088640 | bytes 11272192 | tf_op jit(solution)/shard_map/dot_general | solution.py:173
  285.2 2.4 collective-permute-start.6
  287.6 2.1 collective-permute-start.7
  289.7 3.9 %collective-permute-start.8 = (bf16[64,64,10]{1,0,2:T(8,128)(2,1)S(1)}, bf16[64,64,10]{1,0,2:T(8,128)(2,1)S(1)}, u32[]{:S(2)}, u32[]{:S(2)}) collective-permute-start(bf16[64,64,10]{1,0,2:T(8,128)(2,1)S(1)} %get-tuple-element.146), channel_id=1, source_target_pairs={{0,3},{1,4},{2,5},{3,6},{4,7},{5,0},{6,1},{7,2},{8,11},{9,12},{10,... | collective-permute-start | bytes 245768 | tf_op jit(solution)/shard_map/ppermute | solution.py:22
  293.6 5.1 %collective-permute-start.9 = (bf16[64,64,10]{1,0,2:T(8,128)(2,1)S(1)}, bf16[64,64,10]{1,0,2:T(8,128)(2,1)S(1)}, u32[]{:S(2)}, u32[]{:S(2)}) collective-permute-start(bf16[64,64,10]{1,0,2:T(8,128)(2,1)S(1)} %get-tuple-element.146), channel_id=1, source_target_pairs={{0,4},{1,5},{2,6},{3,7},{4,0},{5,1},{6,2},{7,3},{8,12},{9,13},{10,... | collective-permute-start | bytes 245768 | tf_op jit(solution)/shard_map/ppermute | solution.py:22
  298.7 3.0 collective-permute-start.10
  301.8 4.3 %collective-permute-start.11 = (bf16[64,64,10]{1,0,2:T(8,128)(2,1)S(1)}, bf16[64,64,10]{1,0,2:T(8,128)(2,1)S(1)}, u32[]{:S(2)}, u32[]{:S(2)}) collective-permute-start(bf16[64,64,10]{1,0,2:T(8,128)(2,1)S(1)} %get-tuple-element.146), channel_id=1, source_target_pairs={{0,6},{1,7},{2,0},{3,1},{4,2},{5,3},{6,4},{7,5},{8,14},{9,15},{10,... | collective-permute-start | bytes 245768 | tf_op jit(solution)/shard_map/ppermute | solution.py:22
  306.2 2.5 collective-permute-start.12
  308.7 1.8 collective-permute-done.8
  310.5 3.1 collective-permute-done.9
  313.6 2.0 collective-permute-done.10
  315.7 8.4 %collective-permute-done.11 = bf16[64,64,10]{1,0,2:T(8,128)(2,1)S(1)} collective-permute-done((bf16[64,64,10]{1,0,2:T(8,128)(2,1)S(1)}, bf16[64,64,10]{1,0,2:T(8,128)(2,1)S(1)}, u32[]{:S(2)}, u32[]{:S(2)}) %collective-permute-start.11) | collective-permute-done | bytes 81952 | tf_op jit(solution)/shard_map/ppermute | solution.py:22
  324.1 4.9 %collective-permute-done.12 = bf16[64,64,10]{1,0,2:T(8,128)(2,1)S(1)} collective-permute-done((bf16[64,64,10]{1,0,2:T(8,128)(2,1)S(1)}, bf16[64,64,10]{1,0,2:T(8,128)(2,1)S(1)}, u32[]{:S(2)}, u32[]{:S(2)}) %collective-permute-start.12) | collective-permute-done | bytes 81952 | tf_op jit(solution)/shard_map/ppermute | solution.py:22
  331.1 3.5 %copy.43 = bf16[64,64,8,10]{0,3,2,1:T(8,128)(2,1)S(1)} copy(bf16[64,64,8,10]{1,0,3,2:T(8,128)(2,1)} %select_bitcast_fusion) | data formatting | bytes 1310720 | tf_op jit(solution)/shard_map/jit(_take)/select_n | solution.py:180
  (98 shorter events, 15.2 us)
Async XLA Ops:
  0.0 45.9 %copy-start = (s32[32,32]{1,0:T(8,128)S(1)}, s32[32,32]{1,0:T(8,128)}, u32[]{:S(2)}) copy-start(s32[32,32]{1,0:T(8,128)} %param.16) | copy-start | bytes 12292
  21.0 15.5 %copy-start.1 = (bf16[64,640]{1,0:T(8,128)(2,1)S(1)}, bf16[64,640]{1,0:T(8,128)(2,1)}, u32[]{:S(2)}) copy-start(bf16[64,640]{1,0:T(8,128)(2,1)} %param.10) | copy-start | bytes 245764
  21.0 15.6 %copy-start.4 = (s32[32]{0:T(128)S(1)}, s32[32]{0:T(128)}, u32[]{:S(2)}) copy-start(s32[32]{0:T(128)} %param.15) | copy-start | bytes 388
  21.0 16.9 %copy-start.2 = (bf16[64,128]{1,0:T(8,128)(2,1)S(1)}, bf16[64,128]{1,0:T(8,128)(2,1)}, u32[]{:S(2)}) copy-start(bf16[64,128]{1,0:T(8,128)(2,1)} %param.11) | copy-start | bytes 49156
  21.0 248.3 %all-to-all-start.1 = ((bf16[64,16,5120]{2,1,0:T(8,128)(2,1)}), bf16[64,16,5120]{2,1,0:T(8,128)(2,1)}, u32[]{:S(2)}, u32[]{:S(2)}) async-start(bf16[64,16,5120]{2,1,0:T(8,128)(2,1)} %stack.20), calls=%async_computation.1 | async-start | bytes 20971520 | tf_op jit(solution)/shard_map/all_to_all | solution.py:66
  36.6 6.4 %copy-start.3 = (bf16[64,128]{1,0:T(8,128)(2,1)S(1)}, bf16[64,128]{1,0:T(8,128)(2,1)}, u32[]{:S(2)}) copy-start(bf16[64,128]{1,0:T(8,128)(2,1)} %param.12) | copy-start | bytes 49156
  38.6 7.5 %collective-permute-start.1 = (bf16[64,5,128]{2,1,0:T(8,128)(2,1)S(1)}, bf16[64,5,128]{2,1,0:T(8,128)(2,1)S(1)}, u32[]{:S(2)}, u32[]{:S(2)}) collective-permute-start(bf16[64,5,128]{2,1,0:T(8,128)(2,1)S(1)} %fusion.28), channel_id=1, source_target_pairs={{0,8},{8,0},{16,24},{24,16},{32,40},{40,32},{48,56},{56,48},{64,72... | collective-permute-start | bytes 245768 | tf_op jit(solution)/shard_map/ppermute | solution.py:15
  40.9 5.3 %collective-permute-start = (bf16[64,1,128]{2,0,1:T(8,128)(2,1)S(1)}, bf16[64,1,128]{2,0,1:T(8,128)(2,1)S(1)}, u32[]{:S(2)}, u32[]{:S(2)}) collective-permute-start(bf16[64,1,128]{2,0,1:T(8,128)(2,1)S(1)} %bitcast.180), channel_id=1, source_target_pairs={{0,8},{8,0},{16,24},{24,16},{32,40},{40,32},{48,56},{56,48},{64,72... | collective-permute-start | bytes 49160 | tf_op jit(solution)/shard_map/ppermute | solution.py:15
  42.9 3.8 %collective-permute-start.2 = (bf16[64,1,128]{2,0,1:T(8,128)(2,1)S(1)}, bf16[64,1,128]{2,0,1:T(8,128)(2,1)S(1)}, u32[]{:S(2)}, u32[]{:S(2)}) collective-permute-start(bf16[64,1,128]{2,0,1:T(8,128)(2,1)S(1)} %bitcast.181), channel_id=1, source_target_pairs={{0,8},{8,0},{16,24},{24,16},{32,40},{40,32},{48,56},{56,48},{64,72... | collective-permute-start | bytes 49160 | tf_op jit(solution)/shard_map/ppermute | solution.py:15
  62.8 6.6 %collective-permute-start.3 = (bf16[1,5,64]{2,1,0:T(8,128)(2,1)S(1)}, bf16[1,5,64]{2,1,0:T(8,128)(2,1)S(1)}, u32[]{:S(2)}, u32[]{:S(2)}) collective-permute-start(bf16[1,5,64]{2,1,0:T(8,128)(2,1)S(1)} %dynamic-slice_convert_fusion.2), channel_id=1, source_target_pairs={{0,8},{8,0},{16,24},{24,16},{32,40},{40,32},{48,56},{56,48},{64,72... | collective-permute-start | bytes 1928 | tf_op jit(solution)/shard_map/ppermute | solution.py:15
  64.9 4.5 %collective-permute-start.5 = (bf16[1,5,64]{2,1,0:T(8,128)(2,1)S(1)}, bf16[1,5,64]{2,1,0:T(8,128)(2,1)S(1)}, u32[]{:S(2)}, u32[]{:S(2)}) collective-permute-start(bf16[1,5,64]{2,1,0:T(8,128)(2,1)S(1)} %dynamic-slice_convert_fusion.1), channel_id=1, source_target_pairs={{0,8},{8,0},{16,24},{24,16},{32,40},{40,32},{48,56},{56,48},{64,72... | collective-permute-start | bytes 1928 | tf_op jit(solution)/shard_map/ppermute | solution.py:15
  67.3 3.3 collective-permute-start.4
  285.2 16.6 %collective-permute-start.6 = (bf16[64,64,10]{1,0,2:T(8,128)(2,1)S(1)}, bf16[64,64,10]{1,0,2:T(8,128)(2,1)S(1)}, u32[]{:S(2)}, u32[]{:S(2)}) collective-permute-start(bf16[64,64,10]{1,0,2:T(8,128)(2,1)S(1)} %get-tuple-element.146), channel_id=1, source_target_pairs={{0,1},{1,2},{2,3},{3,4},{4,5},{5,6},{6,7},{7,0},{8,9},{9,10},{10,1... | collective-permute-start | bytes 245768 | tf_op jit(solution)/shard_map/ppermute | solution.py:22
  287.6 18.6 %collective-permute-start.7 = (bf16[64,64,10]{1,0,2:T(8,128)(2,1)S(1)}, bf16[64,64,10]{1,0,2:T(8,128)(2,1)S(1)}, u32[]{:S(2)}, u32[]{:S(2)}) collective-permute-start(bf16[64,64,10]{1,0,2:T(8,128)(2,1)S(1)} %get-tuple-element.146), channel_id=1, source_target_pairs={{0,2},{1,3},{2,4},{3,5},{4,6},{5,7},{6,0},{7,1},{8,10},{9,11},{10,... | collective-permute-start | bytes 245768 | tf_op jit(solution)/shard_map/ppermute | solution.py:22
  289.7 20.8 %collective-permute-start.8 = (bf16[64,64,10]{1,0,2:T(8,128)(2,1)S(1)}, bf16[64,64,10]{1,0,2:T(8,128)(2,1)S(1)}, u32[]{:S(2)}, u32[]{:S(2)}) collective-permute-start(bf16[64,64,10]{1,0,2:T(8,128)(2,1)S(1)} %get-tuple-element.146), channel_id=1, source_target_pairs={{0,3},{1,4},{2,5},{3,6},{4,7},{5,0},{6,1},{7,2},{8,11},{9,12},{10,... | collective-permute-start | bytes 245768 | tf_op jit(solution)/shard_map/ppermute | solution.py:22
  293.6 20.0 %collective-permute-start.9 = (bf16[64,64,10]{1,0,2:T(8,128)(2,1)S(1)}, bf16[64,64,10]{1,0,2:T(8,128)(2,1)S(1)}, u32[]{:S(2)}, u32[]{:S(2)}) collective-permute-start(bf16[64,64,10]{1,0,2:T(8,128)(2,1)S(1)} %get-tuple-element.146), channel_id=1, source_target_pairs={{0,4},{1,5},{2,6},{3,7},{4,0},{5,1},{6,2},{7,3},{8,12},{9,13},{10,... | collective-permute-start | bytes 245768 | tf_op jit(solution)/shard_map/ppermute | solution.py:22
  298.7 16.9 %collective-permute-start.10 = (bf16[64,64,10]{1,0,2:T(8,128)(2,1)S(1)}, bf16[64,64,10]{1,0,2:T(8,128)(2,1)S(1)}, u32[]{:S(2)}, u32[]{:S(2)}) collective-permute-start(bf16[64,64,10]{1,0,2:T(8,128)(2,1)S(1)} %get-tuple-element.146), channel_id=1, source_target_pairs={{0,5},{1,6},{2,7},{3,0},{4,1},{5,2},{6,3},{7,4},{8,13},{9,14},{10,... | collective-permute-start | bytes 245768 | tf_op jit(solution)/shard_map/ppermute | solution.py:22
  301.8 22.3 %collective-permute-start.11 = (bf16[64,64,10]{1,0,2:T(8,128)(2,1)S(1)}, bf16[64,64,10]{1,0,2:T(8,128)(2,1)S(1)}, u32[]{:S(2)}, u32[]{:S(2)}) collective-permute-start(bf16[64,64,10]{1,0,2:T(8,128)(2,1)S(1)} %get-tuple-element.146), channel_id=1, source_target_pairs={{0,6},{1,7},{2,0},{3,1},{4,2},{5,3},{6,4},{7,5},{8,14},{9,15},{10,... | collective-permute-start | bytes 245768 | tf_op jit(solution)/shard_map/ppermute | solution.py:22
  306.2 22.8 %collective-permute-start.12 = (bf16[64,64,10]{1,0,2:T(8,128)(2,1)S(1)}, bf16[64,64,10]{1,0,2:T(8,128)(2,1)S(1)}, u32[]{:S(2)}, u32[]{:S(2)}) collective-permute-start(bf16[64,64,10]{1,0,2:T(8,128)(2,1)S(1)} %get-tuple-element.146), channel_id=1, source_target_pairs={{0,7},{1,0},{2,1},{3,2},{4,3},{5,4},{6,5},{7,6},{8,15},{9,8},{10,9... | collective-permute-start | bytes 245768 | tf_op jit(solution)/shard_map/ppermute | solution.py:22
